TPU v7x, 32 devices: a whole 2x2x4 slice. The times are simulated.
32 devices in a mesh: test: 4 (over z), cell: 8 (over y, x, core).
Axes of the slice: x: 2, y: 2, z: 4, core: 2. Of those that a mesh axis runs over, the one named last changes fastest.
Arguments:
- log_perm: float32 [128, 16, 256], P('cell'), may hold values from -1 to 1
- panel: float32 [8, 128, 16, 256], P('test', 'cell'), may hold values from -4 to 4
- wells: int32 [4, 8], P('test'), may hold values from 0 to 524287
- rates: float32 [4, 8], P('test'), may hold values from 1 to 10
- recharge: float32 [4, 128, 16, 256], P('test', 'cell'), may hold values from 0.25 to 4
- gauge: float32 [128, 16, 256], P('cell'), may hold values from 0.25 to 4
Outputs:
- hessian_panel: float32 [8, 128, 16, 256], P('test', 'cell')
Inputs may be any that keep to these rules, and one draw needn't show every extreme that they name: `wells`: each entry names a cell of the whole grid, numbered x * 16 * 256 + y * 256 + z; a test may name a cell more than once.
All inputs are finite; a program needn't handle non-finite values.
Results may differ from a plain program's by a relative error of at most 0.0001.
Values sent between devices are 32-bit elements; how exact they have to be, the bound alone decides.
No kernel may reach another device: no remote copies, remote signals or barrier semaphores. Data moves between devices by JAX's collectives and lax.ppermute only.
A program may use at most 64 MiB of HBM per device.

v0:
```python
import math
import jax
import jax.numpy as jnp
import numpy as np
from jax import lax
from jax.sharding import PartitionSpec as P

CHEB = 4
storage = 0.02


def with_halo(cells, sides, width):
    for axis, dim in sides:
        count = lax.axis_size(axis)
        ends = count - 1
        head = lax.slice_in_dim(cells, 0, width, axis=dim)
        tail = lax.slice_in_dim(cells, cells.shape[dim] - width, cells.shape[dim], axis=dim)
        cells = jnp.concatenate(
            [
                lax.ppermute(tail, axis, [(i, (i + 1) % count) for i in range(ends)]),
                cells,
                lax.ppermute(head, axis, [((i + 1) % count, i) for i in range(ends)]),
            ],
            axis=dim,
        )
    return cells


def cheb_table(count):
    highest = storage + 12.0 * math.e
    theta = 0.5 * (highest + storage)
    spread = 0.5 * (highest - storage)
    sigma = theta / spread
    rho = 1.0 / sigma
    keeps = []
    pushes = []
    for turn in range(count):
        after = 1.0 / (2.0 * sigma - rho)
        keeps.append(after * rho)
        pushes.append(2.0 * after / spread)
        rho = after
    return (1.0 / theta, keeps, pushes)


def neighbours(field, back):
    axis = field.ndim - back
    widths = [(0, 0)] * field.ndim
    widths[axis] = (1, 1)
    padded = jnp.pad(field, widths)
    length = field.shape[axis]
    return (
        lax.slice_in_dim(padded, 2, length + 2, axis=axis),
        lax.slice_in_dim(padded, 0, length, axis=axis),
    )


def diffuse(weight_ext, field_ext):
    weight = weight_ext[..., 1:-1, :, :]
    field = field_ext[..., 1:-1, :, :]
    total = 0.5 * (weight + weight_ext[..., 2:, :, :]) * (field - field_ext[..., 2:, :, :])
    total = total + 0.5 * (weight + weight_ext[..., :-2, :, :]) * (
        field - field_ext[..., :-2, :, :]
    )
    for back in (2, 1):
        weight_up, weight_down = neighbours(weight, back)
        field_up, field_down = neighbours(field, back)
        total = (
            total
            + 0.5 * (weight + weight_up) * (field - field_up)
            + 0.5 * (weight + weight_down) * (field - field_down)
        )
    return total


def pairs(left_ext, right_ext):
    left = left_ext[..., 1:-1, :, :]
    right = right_ext[..., 1:-1, :, :]
    total = (left - left_ext[..., 2:, :, :]) * (right - right_ext[..., 2:, :, :])
    total = total + (left - left_ext[..., :-2, :, :]) * (right - right_ext[..., :-2, :, :])
    for back in (2, 1):
        left_up, left_down = neighbours(left, back)
        right_up, right_down = neighbours(right, back)
        total = (
            total
            + (left - left_up) * (right - right_up)
            + (left - left_down) * (right - right_down)
        )
    return total


def rims(field):
    return with_halo(field, (("cell", 1),), 1)


def shards(log_perm, panel, wells, rates, recharge, gauge):
    place = lax.axis_index("cell")
    slab, rows_y, depth_z = log_perm.shape
    tests_here, well_count = wells.shape
    first, keeps, pushes = cheb_table(CHEB)
    keep_table = jnp.asarray(np.array(keeps, np.float32))
    push_table = jnp.asarray(np.array(pushes, np.float32))
    columns = lax.all_gather(panel, "test", axis=0, tiled=True)
    columns_all = columns.shape[0]
    perm = jnp.exp(log_perm)
    stacked = jnp.concatenate([perm[None], perm[None] * columns], axis=0)
    coeff_ext = with_halo(stacked, (("cell", 1),), 2)
    perm_ext = coeff_ext[0]
    scaled_ext = coeff_ext[1:, 1:-1]
    cells = slab * rows_y * depth_z
    flat = place * cells + jnp.arange(cells, dtype=jnp.int32)
    hits = wells[:, :, None] == flat[None, None, :]
    points = jnp.sum(jnp.where(hits, rates[:, :, None], 0.0), axis=1).reshape(
        tests_here, slab, rows_y, depth_z
    )
    counts = jnp.sum(hits.astype(jnp.float32), axis=1).reshape(tests_here, slab, rows_y, depth_z)
    source = recharge + points
    observe = gauge[None] + counts

    def solve(right_side):
        solution = jnp.zeros_like(right_side)
        residual = right_side
        direction = right_side * first

        def sweep(turn, carry):
            solution, residual, direction = carry
            extended = with_halo(direction, (("cell", 1),), 1)
            image = storage * direction + diffuse(perm_ext[1:-1], extended)
            solution = solution + direction
            residual = residual - image
            direction = keep_table[turn] * direction + push_table[turn] * residual
            return (solution, residual, direction)

        solution, residual, direction = lax.fori_loop(
            0, CHEB, sweep, (solution, residual, direction)
        )
        return solution + direction

    state = solve(source)
    state_ext = rims(state)
    forcing = -diffuse(scaled_ext, state_ext[:, None])
    forcing = forcing.reshape(tests_here * columns_all, slab, rows_y, depth_z)
    change = solve(forcing)
    weighted = (
        change.reshape(tests_here, columns_all, slab, rows_y, depth_z) * observe[:, None]
    ).reshape(tests_here * columns_all, slab, rows_y, depth_z)
    adjoint = solve(weighted)
    adjoint_ext = rims(adjoint).reshape(tests_here, columns_all, slab + 2, rows_y, depth_z)
    contrib = jnp.sum(pairs(state_ext[:, None], adjoint_ext), axis=0)
    partial_value = -0.5 * perm[None] * contrib
    total = lax.psum(partial_value, "test")
    share = panel.shape[0]
    owned = lax.dynamic_slice_in_dim(total, lax.axis_index("test") * share, share, 0)
    return owned


def solution(mesh):
    return jax.shard_map(
        shards,
        mesh=mesh,
        in_specs=(
            P("cell", None, None),
            P("test", "cell", None, None),
            P("test", None),
            P("test", None),
            P("test", "cell", None, None),
            P("cell", None, None),
        ),
        out_specs=P("test", "cell", None, None),
        check_vma=False,
    )
```

profile of v0, /device:TPU:0, one launch (start us, length us, event | category | flops | bytes accessed | tf_op | source)
XLA Modules:
  0.0 408.5 jit_solution(683576134354521020)
XLA Ops:
  7.3 1.7 broadcast_multiply_fusion.14
  9.1 48.2 %all-gather.2.cloned.1.call-done = f32[8,16,16,256]{3,2,1,0:T(8,128)} async-done(((f32[2,16,16,256]{3,2,1,0:T(8,128)}), f32[8,16,16,256]{3,2,1,0:T(8,128)}) %all-gather.2.cloned.1.call-update) | async-done | bytes 2097168 | tf_op jit(solution)/shard_map/all_gather | solution.py:102
  57.3 2.0 broadcast_multiply_fusion.6
  61.4 3.0 collective-permute-start.7
  64.5 1.7 fusion.86
  66.3 1.8 broadcast_multiply_fusion.13
  70.8 51.1 %while.63 = (s32[]{:T(128)}, f32[1,16,16,256]{3,2,1,0:T(8,128)}, f32[1,16,16,256]{3,2,1,0:T(8,128)}, f32[1,16,16,256]{3,2,1,0:T(8,128)}, f32[16,16,256]{2,1,0:T(...) while((s32[]{:T(128)}, f32[1,16,16,256]{3,2,1,0:T(8,128)}, ...), condition=%wide.region_2.3_spmd.clone.clone, body=%wide.region_1.2_spmd.sunk.clone.clone.sunk | while | flops 2424835 | bytes 3637479 | solution.py:133
  71.7 3.3 collective-permute-start
  77.6 2.4 collective-permute-done.1
  80.0 3.5 multiply_add_fusion.6
  84.4 4.4 %collective-permute-start = (f32[1,1,16,256]{3,2,1,0:T(8,128)S(1)}, f32[1,1,16,256]{3,2,1,0:T(8,128)S(1)}, u32[]{:S(2)}, u32[]{:S(2)}) collective-permute-start(f32[1,1,16,256]{3,2,1,0:T(8,128)S(1)} %get-tuple-element.979), channel_id=1, source_target_pairs={{0,1},{1,2},{2,3},{3,4},{4,5},{5,6},{6,7},{8,9},{9,10},{10,11},{11... | collective-permute-start | bytes 49160 | tf_op jit(solution)/shard_map/while/body/eval_jaxpr/ppermute | solution.py:20
  92.1 3.6 multiply_add_fusion.6
  96.7 6.0 %collective-permute-start = (f32[1,1,16,256]{3,2,1,0:T(8,128)S(1)}, f32[1,1,16,256]{3,2,1,0:T(8,128)S(1)}, u32[]{:S(2)}, u32[]{:S(2)}) collective-permute-start(f32[1,1,16,256]{3,2,1,0:T(8,128)S(1)} %get-tuple-element.979), channel_id=1, source_target_pairs={{0,1},{1,2},{2,3},{3,4},{4,5},{5,6},{6,7},{8,9},{9,10},{10,11},{11... | collective-permute-start | bytes 49160 | tf_op jit(solution)/shard_map/while/body/eval_jaxpr/ppermute | solution.py:20
  105.8 3.6 multiply_add_fusion.6
  110.3 4.8 %collective-permute-start = (f32[1,1,16,256]{3,2,1,0:T(8,128)S(1)}, f32[1,1,16,256]{3,2,1,0:T(8,128)S(1)}, u32[]{:S(2)}, u32[]{:S(2)}) collective-permute-start(f32[1,1,16,256]{3,2,1,0:T(8,128)S(1)} %get-tuple-element.979), channel_id=1, source_target_pairs={{0,1},{1,2},{2,3},{3,4},{4,5},{5,6},{6,7},{8,9},{9,10},{10,11},{11... | collective-permute-start | bytes 49160 | tf_op jit(solution)/shard_map/while/body/eval_jaxpr/ppermute | solution.py:20
  118.2 3.6 multiply_add_fusion.6
  122.9 4.8 %collective-permute-start.8 = (f32[1,1,16,256]{3,2,1,0:T(8,128)S(1)}, f32[1,1,16,256]{3,2,1,0:T(8,128)S(1)}, u32[]{:S(2)}, u32[]{:S(2)}) collective-permute-start(f32[1,1,16,256]{3,2,1,0:T(8,128)S(1)} %get-tuple-element.831), channel_id=1, source_target_pairs={{0,1},{1,2},{2,3},{3,4},{4,5},{5,6},{6,7},{8,9},{9,10},{10,11},{11... | collective-permute-start | bytes 49160 | tf_op jit(solution)/shard_map/ppermute | solution.py:20
  130.1 1.7 add.631
  133.3 4.0 broadcast_multiply_fusion.5
  137.3 76.5 %while.64 = (s32[]{:T(128)}, f32[8,16,16,256]{3,2,1,0:T(8,128)}, f32[8,16,16,256]{3,2,1,0:T(8,128)}, f32[8,16,16,256]{3,2,1,0:T(8,128)}, f32[16,16,256]{2,1,0:T(...) while((s32[]{:T(128)}, f32[8,16,16,256]{3,2,1,0:T(8,128)}, ...), condition=%wide.region_4.5_spmd.clone.clone, body=%wide.region_3.4_spmd.sunk.clone.clone.sunk | while | flops 14811139 | bytes 23068904 | solution.py:133
  139.6 4.5 %collective-permute-start.2 = (f32[8,1,16,256]{3,2,1,0:T(8,128)}, f32[8,1,16,256]{3,2,1,0:T(8,128)}, u32[]{:S(2)}, u32[]{:S(2)}) collective-permute-start(f32[8,1,16,256]{3,2,1,0:T(8,128)} %get-tuple-element.995), channel_id=1, source_target_pairs={{0,1},{1,2},{2,3},{3,4},{4,5},{5,6},{6,7},{8,9},{9,10},{10,11},{11... | collective-permute-start | bytes 393224 | tf_op jit(solution)/shard_map/while/body/eval_jaxpr/ppermute | solution.py:20
  147.8 7.1 %multiply_add_fusion.7 = (f32[8,16,16,256]{3,2,1,0:T(8,128)}, f32[8,16,16,256]{3,2,1,0:T(8,128)}, f32[8,16,16,256]{3,2,1,0:T(8,128)}) fusion(f32[8,16,16,256]{3,2,1,0:T(8,128)S(1)} %copy.50, f32[]{:T(128)} %bitcast.98, f32[]{:T(128)} %bitcast.99, f32[8,16,16,256]{3,2,1,0:T(8,128)} %get-tuple-element.1066, f32[16,16,256]{2,1,0:T(8,128)S(1)} %get-tuple-element.991, ...), kind=kLoop, calls=%fused_computation.69.clone.1 | loop fusion | flops 14155776 | bytes 14417929 | tf_op jit(solution)/shard_map/while/body/eval_jaxpr/add | solution.py:130
  154.9 1.6 copy.50
  157.3 6.1 %collective-permute-start.2 = (f32[8,1,16,256]{3,2,1,0:T(8,128)}, f32[8,1,16,256]{3,2,1,0:T(8,128)}, u32[]{:S(2)}, u32[]{:S(2)}) collective-permute-start(f32[8,1,16,256]{3,2,1,0:T(8,128)} %get-tuple-element.995), channel_id=1, source_target_pairs={{0,1},{1,2},{2,3},{3,4},{4,5},{5,6},{6,7},{8,9},{9,10},{10,11},{11... | collective-permute-start | bytes 393224 | tf_op jit(solution)/shard_map/while/body/eval_jaxpr/ppermute | solution.py:20
  167.0 7.5 %multiply_add_fusion.7 = (f32[8,16,16,256]{3,2,1,0:T(8,128)}, f32[8,16,16,256]{3,2,1,0:T(8,128)}, f32[8,16,16,256]{3,2,1,0:T(8,128)}) fusion(f32[8,16,16,256]{3,2,1,0:T(8,128)S(1)} %copy.50, f32[]{:T(128)} %bitcast.98, f32[]{:T(128)} %bitcast.99, f32[8,16,16,256]{3,2,1,0:T(8,128)} %get-tuple-element.1066, f32[16,16,256]{2,1,0:T(8,128)S(1)} %get-tuple-element.991, ...), kind=kLoop, calls=%fused_computation.69.clone.1 | loop fusion | flops 14155776 | bytes 14417929 | tf_op jit(solution)/shard_map/while/body/eval_jaxpr/add | solution.py:130
  174.4 1.6 copy.50
  176.7 6.7 %collective-permute-start.2 = (f32[8,1,16,256]{3,2,1,0:T(8,128)}, f32[8,1,16,256]{3,2,1,0:T(8,128)}, u32[]{:S(2)}, u32[]{:S(2)}) collective-permute-start(f32[8,1,16,256]{3,2,1,0:T(8,128)} %get-tuple-element.995), channel_id=1, source_target_pairs={{0,1},{1,2},{2,3},{3,4},{4,5},{5,6},{6,7},{8,9},{9,10},{10,11},{11... | collective-permute-start | bytes 393224 | tf_op jit(solution)/shard_map/while/body/eval_jaxpr/ppermute | solution.py:20
  187.1 7.5 %multiply_add_fusion.7 = (f32[8,16,16,256]{3,2,1,0:T(8,128)}, f32[8,16,16,256]{3,2,1,0:T(8,128)}, f32[8,16,16,256]{3,2,1,0:T(8,128)}) fusion(f32[8,16,16,256]{3,2,1,0:T(8,128)S(1)} %copy.50, f32[]{:T(128)} %bitcast.98, f32[]{:T(128)} %bitcast.99, f32[8,16,16,256]{3,2,1,0:T(8,128)} %get-tuple-element.1066, f32[16,16,256]{2,1,0:T(8,128)S(1)} %get-tuple-element.991, ...), kind=kLoop, calls=%fused_computation.69.clone.1 | loop fusion | flops 14155776 | bytes 14417929 | tf_op jit(solution)/shard_map/while/body/eval_jaxpr/add | solution.py:130
  194.5 1.6 copy.50
  196.8 5.8 %collective-permute-start.2 = (f32[8,1,16,256]{3,2,1,0:T(8,128)}, f32[8,1,16,256]{3,2,1,0:T(8,128)}, u32[]{:S(2)}, u32[]{:S(2)}) collective-permute-start(f32[8,1,16,256]{3,2,1,0:T(8,128)} %get-tuple-element.995), channel_id=1, source_target_pairs={{0,1},{1,2},{2,3},{3,4},{4,5},{5,6},{6,7},{8,9},{9,10},{10,11},{11... | collective-permute-start | bytes 393224 | tf_op jit(solution)/shard_map/while/body/eval_jaxpr/ppermute | solution.py:20
  206.3 7.5 %multiply_add_fusion.7 = (f32[8,16,16,256]{3,2,1,0:T(8,128)}, f32[8,16,16,256]{3,2,1,0:T(8,128)}, f32[8,16,16,256]{3,2,1,0:T(8,128)}) fusion(f32[8,16,16,256]{3,2,1,0:T(8,128)S(1)} %copy.50, f32[]{:T(128)} %bitcast.98, f32[]{:T(128)} %bitcast.99, f32[8,16,16,256]{3,2,1,0:T(8,128)} %get-tuple-element.1066, f32[16,16,256]{2,1,0:T(8,128)S(1)} %get-tuple-element.991, ...), kind=kLoop, calls=%fused_computation.69.clone.1 | loop fusion | flops 14155776 | bytes 14417929 | tf_op jit(solution)/shard_map/while/body/eval_jaxpr/add | solution.py:130
  213.7 4.9 %broadcast_multiply_fusion.4 = (f32[8,16,16,256]{3,2,1,0:T(8,128)}, f32[8,16,16,256]{3,2,1,0:T(8,128)}) fusion(f32[16,16,256]{2,1,0:T(8,128)} %add.631, f32[8,16,16,256]{3,2,1,0:T(8,128)} %get-tuple-element.571, f32[8,16,16,256]{3,2,1,0:T(8,128)} %get-tuple-element.572), kind=kLoop, calls=%fused_computation.180 | loop fusion | flops 1572864 | bytes 8650752 | tf_op jit(solution)/shard_map/mul | solution.py:122
  218.7 75.9 %while.65 = (s32[]{:T(128)}, f32[8,16,16,256]{3,2,1,0:T(8,128)}, f32[8,16,16,256]{3,2,1,0:T(8,128)}, f32[8,16,16,256]{3,2,1,0:T(8,128)}, f32[16,16,256]{2,1,0:T(...) while((s32[]{:T(128)}, f32[8,16,16,256]{3,2,1,0:T(8,128)}, ...), condition=%wide.region_7.8_spmd.clone.clone, body=%wide.region_6.7_spmd.sunk.clone.clone.sunk | while | flops 14811139 | bytes 23068904 | solution.py:133
  218.7 1.6 copy.51
  221.0 5.8 %collective-permute-start.4 = (f32[8,1,16,256]{3,2,1,0:T(8,128)}, f32[8,1,16,256]{3,2,1,0:T(8,128)}, u32[]{:S(2)}, u32[]{:S(2)}) collective-permute-start(f32[8,1,16,256]{3,2,1,0:T(8,128)} %get-tuple-element.1013), channel_id=1, source_target_pairs={{0,1},{1,2},{2,3},{3,4},{4,5},{5,6},{6,7},{8,9},{9,10},{10,11},{11... | collective-permute-start | bytes 393224 | tf_op jit(solution)/shard_map/while/body/eval_jaxpr/ppermute | solution.py:20
  230.3 7.0 %multiply_add_fusion.8 = (f32[8,16,16,256]{3,2,1,0:T(8,128)}, f32[8,16,16,256]{3,2,1,0:T(8,128)}, f32[8,16,16,256]{3,2,1,0:T(8,128)}) fusion(f32[8,16,16,256]{3,2,1,0:T(8,128)S(1)} %copy.51, f32[]{:T(128)} %bitcast.100, f32[]{:T(128)} %bitcast.101, f32[8,16,16,256]{3,2,1,0:T(8,128)} %get-tuple-element.1099, ...), kind=kLoop, calls=%fused_computation.110.clone.1 | loop fusion | flops 14155776 | bytes 14417929 | tf_op jit(solution)/shard_map/while/body/eval_jaxpr/add | solution.py:130
  239.6 5.8 %collective-permute-start.4 = (f32[8,1,16,256]{3,2,1,0:T(8,128)}, f32[8,1,16,256]{3,2,1,0:T(8,128)}, u32[]{:S(2)}, u32[]{:S(2)}) collective-permute-start(f32[8,1,16,256]{3,2,1,0:T(8,128)} %get-tuple-element.1013), channel_id=1, source_target_pairs={{0,1},{1,2},{2,3},{3,4},{4,5},{5,6},{6,7},{8,9},{9,10},{10,11},{11... | collective-permute-start | bytes 393224 | tf_op jit(solution)/shard_map/while/body/eval_jaxpr/ppermute | solution.py:20
  249.1 7.3 %multiply_add_fusion.8 = (f32[8,16,16,256]{3,2,1,0:T(8,128)}, f32[8,16,16,256]{3,2,1,0:T(8,128)}, f32[8,16,16,256]{3,2,1,0:T(8,128)}) fusion(f32[8,16,16,256]{3,2,1,0:T(8,128)S(1)} %copy.51, f32[]{:T(128)} %bitcast.100, f32[]{:T(128)} %bitcast.101, f32[8,16,16,256]{3,2,1,0:T(8,128)} %get-tuple-element.1099, ...), kind=kLoop, calls=%fused_computation.110.clone.1 | loop fusion | flops 14155776 | bytes 14417929 | tf_op jit(solution)/shard_map/while/body/eval_jaxpr/add | solution.py:130
  258.7 5.8 %collective-permute-start.4 = (f32[8,1,16,256]{3,2,1,0:T(8,128)}, f32[8,1,16,256]{3,2,1,0:T(8,128)}, u32[]{:S(2)}, u32[]{:S(2)}) collective-permute-start(f32[8,1,16,256]{3,2,1,0:T(8,128)} %get-tuple-element.1013), channel_id=1, source_target_pairs={{0,1},{1,2},{2,3},{3,4},{4,5},{5,6},{6,7},{8,9},{9,10},{10,11},{11... | collective-permute-start | bytes 393224 | tf_op jit(solution)/shard_map/while/body/eval_jaxpr/ppermute | solution.py:20
  268.1 7.3 %multiply_add_fusion.8 = (f32[8,16,16,256]{3,2,1,0:T(8,128)}, f32[8,16,16,256]{3,2,1,0:T(8,128)}, f32[8,16,16,256]{3,2,1,0:T(8,128)}) fusion(f32[8,16,16,256]{3,2,1,0:T(8,128)S(1)} %copy.51, f32[]{:T(128)} %bitcast.100, f32[]{:T(128)} %bitcast.101, f32[8,16,16,256]{3,2,1,0:T(8,128)} %get-tuple-element.1099, ...), kind=kLoop, calls=%fused_computation.110.clone.1 | loop fusion | flops 14155776 | bytes 14417929 | tf_op jit(solution)/shard_map/while/body/eval_jaxpr/add | solution.py:130
  277.8 5.8 %collective-permute-start.4 = (f32[8,1,16,256]{3,2,1,0:T(8,128)}, f32[8,1,16,256]{3,2,1,0:T(8,128)}, u32[]{:S(2)}, u32[]{:S(2)}) collective-permute-start(f32[8,1,16,256]{3,2,1,0:T(8,128)} %get-tuple-element.1013), channel_id=1, source_target_pairs={{0,1},{1,2},{2,3},{3,4},{4,5},{5,6},{6,7},{8,9},{9,10},{10,11},{11... | collective-permute-start | bytes 393224 | tf_op jit(solution)/shard_map/while/body/eval_jaxpr/ppermute | solution.py:20
  287.2 7.3 %multiply_add_fusion.8 = (f32[8,16,16,256]{3,2,1,0:T(8,128)}, f32[8,16,16,256]{3,2,1,0:T(8,128)}, f32[8,16,16,256]{3,2,1,0:T(8,128)}) fusion(f32[8,16,16,256]{3,2,1,0:T(8,128)S(1)} %copy.51, f32[]{:T(128)} %bitcast.100, f32[]{:T(128)} %bitcast.101, f32[8,16,16,256]{3,2,1,0:T(8,128)} %get-tuple-element.1099, ...), kind=kLoop, calls=%fused_computation.110.clone.1 | loop fusion | flops 14155776 | bytes 14417929 | tf_op jit(solution)/shard_map/while/body/eval_jaxpr/add | solution.py:130
  294.5 2.7 add.632
  297.3 5.2 %collective-permute-start.10 = (f32[8,1,16,256]{3,2,1,0:T(8,128)S(1)}, f32[8,1,16,256]{3,2,1,0:T(8,128)S(1)}, u32[]{:S(2)}, u32[]{:S(2)}) collective-permute-start(f32[8,1,16,256]{3,2,1,0:T(8,128)S(1)} %get-tuple-element.818), channel_id=1, source_target_pairs={{0,1},{1,2},{2,3},{3,4},{4,5},{5,6},{6,7},{8,9},{9,10},{10,11},{11... | collective-permute-start | bytes 393224 | tf_op jit(solution)/shard_map/ppermute | solution.py:20
  303.8 1.9 collective-permute-done.11
  307.5 3.2 fusion.107
  310.7 89.1 %all-reduce.20.cloned.1.call-done = f32[8,16,16,256]{3,2,1,0:T(8,128)} async-done(((f32[8,16,16,256]{3,2,1,0:T(8,128)}), f32[8,16,16,256]{3,2,1,0:T(8,128)}) %all-reduce.20.cloned.1.call-update) | async-done | bytes 2097168 | tf_op jit(solution)/shard_map/psum | solution.py:150
  399.8 1.9 constant_dynamic-slice_fusion
  (170 shorter events, 70.1 us)
Async XLA Ops:
  6.5 50.8 %all-gather.2.cloned.1.call-start = ((), (), s32[]{:S(2)}) async-start(), calls=%async_computation | async-start | bytes 2621440 | tf_op jit(solution)/shard_map/all_gather | solution.py:102
  7.3 392.5 %all-reduce.20.cloned.1.call-start = ((), (), s32[]{:S(2)}) async-start(), calls=%async_computation.1 | async-start | bytes 4194304 | tf_op jit(solution)/shard_map/psum | solution.py:150
  9.0 60.8 %copy-start = (f32[1,16,16,256]{3,2,1,0:T(8,128)}, f32[1,16,16,256]{3,2,1,0:T(8,128)S(1)}, u32[]{:S(2)}) copy-start(f32[1,16,16,256]{3,2,1,0:T(8,128)S(1)} %get-tuple-element.823) | copy-start | bytes 786436
  59.3 5.2 %copy-start.13 = (s32[1,8]{1,0:T(1,128)S(1)}, s32[1,8]{1,0:T(1,128)}, u32[]{:S(2)}) copy-start(s32[1,8]{1,0:T(1,128)} %param.16) | copy-start | bytes 100
  59.3 5.2 %copy-start.14 = (f32[1,8]{1,0:T(1,128)S(1)}, f32[1,8]{1,0:T(1,128)}, u32[]{:S(2)}) copy-start(f32[1,8]{1,0:T(1,128)} %param.17) | copy-start | bytes 100
  60.2 7.9 %collective-permute-start.6 = (f32[9,2,16,256]{3,2,1,0:T(8,128)}, f32[9,2,16,256]{3,2,1,0:T(8,128)S(1)}, u32[]{:S(2)}, u32[]{:S(2)}) collective-permute-start(f32[9,2,16,256]{3,2,1,0:T(8,128)} %get-tuple-element.817), channel_id=1, source_target_pairs={{1,0},{2,1},{3,2},{4,3},{5,4},{6,5},{7,6},{9,8},{10,9},{11,10},{12... | collective-permute-start | bytes 884744 | tf_op jit(solution)/shard_map/ppermute | solution.py:22
  61.4 6.7 %collective-permute-start.7 = (f32[9,2,16,256]{3,2,1,0:T(8,128)}, f32[9,2,16,256]{3,2,1,0:T(8,128)S(1)}, u32[]{:S(2)}, u32[]{:S(2)}) collective-permute-start(f32[9,2,16,256]{3,2,1,0:T(8,128)} %get-tuple-element.816), channel_id=1, source_target_pairs={{0,1},{1,2},{2,3},{3,4},{4,5},{5,6},{6,7},{8,9},{9,10},{10,11},{11... | collective-permute-start | bytes 884744 | tf_op jit(solution)/shard_map/ppermute | solution.py:20
  68.1 2.6 copy-start.2
  69.9 0.8 copy-start.15
  69.9 0.8 copy-start.16
  71.7 5.9 %collective-permute-start = (f32[1,1,16,256]{3,2,1,0:T(8,128)S(1)}, f32[1,1,16,256]{3,2,1,0:T(8,128)S(1)}, u32[]{:S(2)}, u32[]{:S(2)}) collective-permute-start(f32[1,1,16,256]{3,2,1,0:T(8,128)S(1)} %get-tuple-element.979), channel_id=1, source_target_pairs={{0,1},{1,2},{2,3},{3,4},{4,5},{5,6},{6,7},{8,9},{9,10},{10,11},{11... | collective-permute-start | bytes 49160 | tf_op jit(solution)/shard_map/while/body/eval_jaxpr/ppermute | solution.py:20
  75.0 5.0 %collective-permute-start.1 = (f32[1,1,16,256]{3,2,1,0:T(8,128)S(1)}, f32[1,1,16,256]{3,2,1,0:T(8,128)S(1)}, u32[]{:S(2)}, u32[]{:S(2)}) collective-permute-start(f32[1,1,16,256]{3,2,1,0:T(8,128)S(1)} %get-tuple-element.980), channel_id=1, source_target_pairs={{1,0},{2,1},{3,2},{4,3},{5,4},{6,5},{7,6},{9,8},{10,9},{11,10},{12... | collective-permute-start | bytes 49160 | tf_op jit(solution)/shard_map/while/body/eval_jaxpr/ppermute | solution.py:22
  84.4 7.0 %collective-permute-start = (f32[1,1,16,256]{3,2,1,0:T(8,128)S(1)}, f32[1,1,16,256]{3,2,1,0:T(8,128)S(1)}, u32[]{:S(2)}, u32[]{:S(2)}) collective-permute-start(f32[1,1,16,256]{3,2,1,0:T(8,128)S(1)} %get-tuple-element.979), channel_id=1, source_target_pairs={{0,1},{1,2},{2,3},{3,4},{4,5},{5,6},{6,7},{8,9},{9,10},{10,11},{11... | collective-permute-start | bytes 49160 | tf_op jit(solution)/shard_map/while/body/eval_jaxpr/ppermute | solution.py:20
  88.8 3.3 collective-permute-start.1
  96.7 8.6 %collective-permute-start = (f32[1,1,16,256]{3,2,1,0:T(8,128)S(1)}, f32[1,1,16,256]{3,2,1,0:T(8,128)S(1)}, u32[]{:S(2)}, u32[]{:S(2)}) collective-permute-start(f32[1,1,16,256]{3,2,1,0:T(8,128)S(1)} %get-tuple-element.979), channel_id=1, source_target_pairs={{0,1},{1,2},{2,3},{3,4},{4,5},{5,6},{6,7},{8,9},{9,10},{10,11},{11... | collective-permute-start | bytes 49160 | tf_op jit(solution)/shard_map/while/body/eval_jaxpr/ppermute | solution.py:20
  102.7 3.1 collective-permute-start.1
  110.3 7.4 %collective-permute-start = (f32[1,1,16,256]{3,2,1,0:T(8,128)S(1)}, f32[1,1,16,256]{3,2,1,0:T(8,128)S(1)}, u32[]{:S(2)}, u32[]{:S(2)}) collective-permute-start(f32[1,1,16,256]{3,2,1,0:T(8,128)S(1)} %get-tuple-element.979), channel_id=1, source_target_pairs={{0,1},{1,2},{2,3},{3,4},{4,5},{5,6},{6,7},{8,9},{9,10},{10,11},{11... | collective-permute-start | bytes 49160 | tf_op jit(solution)/shard_map/while/body/eval_jaxpr/ppermute | solution.py:20
  115.2 3.1 collective-permute-start.1
  122.9 8.9 %collective-permute-start.8 = (f32[1,1,16,256]{3,2,1,0:T(8,128)S(1)}, f32[1,1,16,256]{3,2,1,0:T(8,128)S(1)}, u32[]{:S(2)}, u32[]{:S(2)}) collective-permute-start(f32[1,1,16,256]{3,2,1,0:T(8,128)S(1)} %get-tuple-element.831), channel_id=1, source_target_pairs={{0,1},{1,2},{2,3},{3,4},{4,5},{5,6},{6,7},{8,9},{9,10},{10,11},{11... | collective-permute-start | bytes 49160 | tf_op jit(solution)/shard_map/ppermute | solution.py:20
  127.7 4.1 collective-permute-start.9
  131.9 1.4 copy-start.1
  131.9 1.4 copy-start.3
  131.9 1.4 copy-start.5
  139.6 8.1 %collective-permute-start.2 = (f32[8,1,16,256]{3,2,1,0:T(8,128)}, f32[8,1,16,256]{3,2,1,0:T(8,128)}, u32[]{:S(2)}, u32[]{:S(2)}) collective-permute-start(f32[8,1,16,256]{3,2,1,0:T(8,128)} %get-tuple-element.995), channel_id=1, source_target_pairs={{0,1},{1,2},{2,3},{3,4},{4,5},{5,6},{6,7},{8,9},{9,10},{10,11},{11... | collective-permute-start | bytes 393224 | tf_op jit(solution)/shard_map/while/body/eval_jaxpr/ppermute | solution.py:20
  144.0 3.8 collective-permute-start.3
  157.3 9.7 %collective-permute-start.2 = (f32[8,1,16,256]{3,2,1,0:T(8,128)}, f32[8,1,16,256]{3,2,1,0:T(8,128)}, u32[]{:S(2)}, u32[]{:S(2)}) collective-permute-start(f32[8,1,16,256]{3,2,1,0:T(8,128)} %get-tuple-element.995), channel_id=1, source_target_pairs={{0,1},{1,2},{2,3},{3,4},{4,5},{5,6},{6,7},{8,9},{9,10},{10,11},{11... | collective-permute-start | bytes 393224 | tf_op jit(solution)/shard_map/while/body/eval_jaxpr/ppermute | solution.py:20
  163.3 3.6 collective-permute-start.3
  176.7 10.3 %collective-permute-start.2 = (f32[8,1,16,256]{3,2,1,0:T(8,128)}, f32[8,1,16,256]{3,2,1,0:T(8,128)}, u32[]{:S(2)}, u32[]{:S(2)}) collective-permute-start(f32[8,1,16,256]{3,2,1,0:T(8,128)} %get-tuple-element.995), channel_id=1, source_target_pairs={{0,1},{1,2},{2,3},{3,4},{4,5},{5,6},{6,7},{8,9},{9,10},{10,11},{11... | collective-permute-start | bytes 393224 | tf_op jit(solution)/shard_map/while/body/eval_jaxpr/ppermute | solution.py:20
  183.4 3.6 collective-permute-start.3
  196.8 9.4 %collective-permute-start.2 = (f32[8,1,16,256]{3,2,1,0:T(8,128)}, f32[8,1,16,256]{3,2,1,0:T(8,128)}, u32[]{:S(2)}, u32[]{:S(2)}) collective-permute-start(f32[8,1,16,256]{3,2,1,0:T(8,128)} %get-tuple-element.995), channel_id=1, source_target_pairs={{0,1},{1,2},{2,3},{3,4},{4,5},{5,6},{6,7},{8,9},{9,10},{10,11},{11... | collective-permute-start | bytes 393224 | tf_op jit(solution)/shard_map/while/body/eval_jaxpr/ppermute | solution.py:20
  202.6 3.6 collective-permute-start.3
  221.0 9.3 %collective-permute-start.4 = (f32[8,1,16,256]{3,2,1,0:T(8,128)}, f32[8,1,16,256]{3,2,1,0:T(8,128)}, u32[]{:S(2)}, u32[]{:S(2)}) collective-permute-start(f32[8,1,16,256]{3,2,1,0:T(8,128)} %get-tuple-element.1013), channel_id=1, source_target_pairs={{0,1},{1,2},{2,3},{3,4},{4,5},{5,6},{6,7},{8,9},{9,10},{10,11},{11... | collective-permute-start | bytes 393224 | tf_op jit(solution)/shard_map/while/body/eval_jaxpr/ppermute | solution.py:20
  226.8 3.6 collective-permute-start.5
  239.6 9.4 %collective-permute-start.4 = (f32[8,1,16,256]{3,2,1,0:T(8,128)}, f32[8,1,16,256]{3,2,1,0:T(8,128)}, u32[]{:S(2)}, u32[]{:S(2)}) collective-permute-start(f32[8,1,16,256]{3,2,1,0:T(8,128)} %get-tuple-element.1013), channel_id=1, source_target_pairs={{0,1},{1,2},{2,3},{3,4},{4,5},{5,6},{6,7},{8,9},{9,10},{10,11},{11... | collective-permute-start | bytes 393224 | tf_op jit(solution)/shard_map/while/body/eval_jaxpr/ppermute | solution.py:20
  245.5 3.6 collective-permute-start.5
  258.7 9.4 %collective-permute-start.4 = (f32[8,1,16,256]{3,2,1,0:T(8,128)}, f32[8,1,16,256]{3,2,1,0:T(8,128)}, u32[]{:S(2)}, u32[]{:S(2)}) collective-permute-start(f32[8,1,16,256]{3,2,1,0:T(8,128)} %get-tuple-element.1013), channel_id=1, source_target_pairs={{0,1},{1,2},{2,3},{3,4},{4,5},{5,6},{6,7},{8,9},{9,10},{10,11},{11... | collective-permute-start | bytes 393224 | tf_op jit(solution)/shard_map/while/body/eval_jaxpr/ppermute | solution.py:20
  264.6 3.6 collective-permute-start.5
  277.8 9.4 %collective-permute-start.4 = (f32[8,1,16,256]{3,2,1,0:T(8,128)}, f32[8,1,16,256]{3,2,1,0:T(8,128)}, u32[]{:S(2)}, u32[]{:S(2)}) collective-permute-start(f32[8,1,16,256]{3,2,1,0:T(8,128)} %get-tuple-element.1013), channel_id=1, source_target_pairs={{0,1},{1,2},{2,3},{3,4},{4,5},{5,6},{6,7},{8,9},{9,10},{10,11},{11... | collective-permute-start | bytes 393224 | tf_op jit(solution)/shard_map/while/body/eval_jaxpr/ppermute | solution.py:20
  283.6 3.6 collective-permute-start.5
  297.3 6.5 %collective-permute-start.10 = (f32[8,1,16,256]{3,2,1,0:T(8,128)S(1)}, f32[8,1,16,256]{3,2,1,0:T(8,128)S(1)}, u32[]{:S(2)}, u32[]{:S(2)}) collective-permute-start(f32[8,1,16,256]{3,2,1,0:T(8,128)S(1)} %get-tuple-element.818), channel_id=1, source_target_pairs={{0,1},{1,2},{2,3},{3,4},{4,5},{5,6},{6,7},{8,9},{9,10},{10,11},{11... | collective-permute-start | bytes 393224 | tf_op jit(solution)/shard_map/ppermute | solution.py:20
  302.5 3.2 collective-permute-start.11
  306.1 1.0 copy-start.6
  306.1 1.0 copy-start.7
  306.1 1.1 copy-start.8
  306.1 1.2 copy-start.9
  306.1 1.2 copy-start.10
  306.1 1.3 copy-start.11
  306.1 1.4 copy-start.12
  (1 other events, 0.8 us)
Sparse Core Ops, SparseCore 0:
  8.9 48.3 all-gather.1
  310.8 88.8 all-reduce.19
where the time goes:
time: 410 us; the launch traced here: 408 us
  waiting for transfers between devices  144 us (35%)
  other arithmetic  110 us (27%)
  starting transfers between devices  97.2 us (24%)
  local copies, waits for them, and re-layouts  42.9 us (10%)
  between operations  13.8 us (3%)
    psum x1, waiting for transfers between devices, shards(): total = lax.psum(partial_value, 'test')  89.1 us
    ppermute x15, starting transfers between devices, with_halo(): lax.ppermute(tail, axis, [(i, (i + 1) % count) for i in range(ends)])  77.9 us
    add x12, other arithmetic, sweep(): direction = keep_table[turn] * direction + push_table[turn] * residual  72.8 us
    all_gather x1, waiting for transfers between devices, shards(): columns = lax.all_gather(panel, 'test', axis=0, tiled=True)  48.2 us
    ppermute x15, starting transfers between devices, with_halo(): lax.ppermute(head, axis, [((i + 1) % count, i) for i in range(ends)])  19.3 us
    while x12, local copies, waits for them, and re-layouts  16.5 us
    dynamic_slice x24, local copies, waits for them, and re-layouts, sweep(): direction = keep_table[turn] * direction + push_table[turn] * residual  15.1 us
    mul x3, other arithmetic, solve(): direction = right_side * first  10.7 us
  transfers between devices with their start and end apart: 32, of which 8 were waited for; matrix products, arithmetic and copies ran while one was open for 8% of the time, Pallas kernels for 0%

commit v1 on v0

--- a/solution.py
+++ b/solution.py
@@ -4,9 +4,19 @@
 import numpy as np
 from jax import lax
 from jax.sharding import PartitionSpec as P
+from jax.lax import axis_size, ppermute
 
 CHEB = 4
 storage = 0.02
+
+
+def ratios_apply(view, row_axis):
+    how_many = axis_size(row_axis)
+    mid_arr = view
+    earlier = lambda r2: [(dev_j, dev_j ^ r2) for dev_j in range(how_many)]
+    for ii in range(how_many.bit_length() - 1):
+        mid_arr = mid_arr + ppermute(mid_arr, row_axis, earlier(1 << ii))
+    return mid_arr
 
 
 def with_halo(cells, sides, width):
@@ -147,7 +157,7 @@
     adjoint_ext = rims(adjoint).reshape(tests_here, columns_all, slab + 2, rows_y, depth_z)
     contrib = jnp.sum(pairs(state_ext[:, None], adjoint_ext), axis=0)
     partial_value = -0.5 * perm[None] * contrib
-    total = lax.psum(partial_value, "test")
+    total = ratios_apply(partial_value, "test")
     share = panel.shape[0]
     owned = lax.dynamic_slice_in_dim(total, lax.axis_index("test") * share, share, 0)
     return owned

time: 410 us -> 463 us (1.13)
  waiting for transfers between devices: 144 us -> 193 us
    ppermute x0 -> x2, waiting for transfers between devices: none -> 138 us  [ratios_apply(): mid_arr = mid_arr + ppermute(mid_arr, row_axis, earlier(1 << ii))]
    psum x1 -> x0, waiting for transfers between devices: 89.1 us -> none  [shards(): total = lax.psum(partial_value, 'test')]
  transfers between devices with their start and end apart: 32 -> 33, of which waited for: 8 -> 9; matrix products, arithmetic and copies ran while one was open for 8% -> 7% of each run, Pallas kernels for 0% -> 0%
where the time goes in v1:
time: 463 us; the launch traced here: 459 us
  waiting for transfers between devices  193 us (42%)
  other arithmetic  112 us (24%)
  starting transfers between devices  98.4 us (21%)
  local copies, waits for them, and re-layouts  41.2 us (9%)
  between operations  13.8 us (3%)
    ppermute x2, waiting for transfers between devices, ratios_apply(): mid_arr = mid_arr + ppermute(mid_arr, row_axis, earlier(1 << ii))  138 us
    ppermute x15, starting transfers between devices, with_halo(): lax.ppermute(tail, axis, [(i, (i + 1) % count) for i in range(ends)])  77.8 us
    add x12, other arithmetic, sweep(): direction = keep_table[turn] * direction + push_table[turn] * residual  73.1 us
    all_gather x1, waiting for transfers between devices, shards(): columns = lax.all_gather(panel, 'test', axis=0, tiled=True)  48.3 us
    ppermute x15, starting transfers between devices, with_halo(): lax.ppermute(head, axis, [((i + 1) % count, i) for i in range(ends)])  19.3 us
    while x12, local copies, waits for them, and re-layouts  16.5 us
    dynamic_slice x24, local copies, waits for them, and re-layouts, sweep(): direction = keep_table[turn] * direction + push_table[turn] * residual  15.2 us
    mul x3, other arithmetic, solve(): direction = right_side * first  10.7 us
  transfers between devices with their start and end apart: 33, of which 9 were waited for; matrix products, arithmetic and copies ran while one was open for 7% of the time, Pallas kernels for 0%

profile of v1, /device:TPU:0, one launch (start us, length us, event | category | flops | bytes accessed | tf_op | source)
XLA Modules:
  0.0 458.5 jit_solution(1333180532528747897)
XLA Ops:
  7.3 1.7 broadcast_multiply_fusion.14
  9.0 48.3 %all-gather.2.cloned.1.call-done = f32[8,16,16,256]{3,2,1,0:T(8,128)} async-done(((f32[2,16,16,256]{3,2,1,0:T(8,128)}), f32[8,16,16,256]{3,2,1,0:T(8,128)}) %all-gather.2.cloned.1.call-update) | async-done | bytes 2097168 | tf_op jit(solution)/shard_map/all_gather | solution.py:112
  57.3 2.0 broadcast_multiply_fusion.6
  61.5 3.0 collective-permute-start.7
  64.5 1.7 fusion.86
  66.3 1.8 broadcast_multiply_fusion.13
  70.7 51.2 %while.63 = (s32[]{:T(128)}, f32[1,16,16,256]{3,2,1,0:T(8,128)}, f32[1,16,16,256]{3,2,1,0:T(8,128)}, f32[1,16,16,256]{3,2,1,0:T(8,128)}, f32[16,16,256]{2,1,0:T(...) while((s32[]{:T(128)}, f32[1,16,16,256]{3,2,1,0:T(8,128)}, ...), condition=%wide.region_2.3_spmd.clone.clone, body=%wide.region_1.2_spmd.sunk.clone.clone.sunk | while | flops 2424835 | bytes 3637479 | solution.py:143
  71.7 3.3 collective-permute-start
  77.6 2.4 collective-permute-done.1
  80.0 3.5 multiply_add_fusion.6
  84.5 4.4 collective-permute-start
  92.1 3.6 multiply_add_fusion.6
  96.7 6.0 %collective-permute-start = (f32[1,1,16,256]{3,2,1,0:T(8,128)S(1)}, f32[1,1,16,256]{3,2,1,0:T(8,128)S(1)}, u32[]{:S(2)}, u32[]{:S(2)}) collective-permute-start(f32[1,1,16,256]{3,2,1,0:T(8,128)S(1)} %get-tuple-element.979), channel_id=1, source_target_pairs={{0,1},{1,2},{2,3},{3,4},{4,5},{5,6},{6,7},{8,9},{9,10},{10,11},{11... | collective-permute-start | bytes 49160 | tf_op jit(solution)/shard_map/while/body/eval_jaxpr/ppermute | solution.py:30
  105.8 3.6 multiply_add_fusion.6
  110.4 4.8 %collective-permute-start = (f32[1,1,16,256]{3,2,1,0:T(8,128)S(1)}, f32[1,1,16,256]{3,2,1,0:T(8,128)S(1)}, u32[]{:S(2)}, u32[]{:S(2)}) collective-permute-start(f32[1,1,16,256]{3,2,1,0:T(8,128)S(1)} %get-tuple-element.979), channel_id=1, source_target_pairs={{0,1},{1,2},{2,3},{3,4},{4,5},{5,6},{6,7},{8,9},{9,10},{10,11},{11... | collective-permute-start | bytes 49160 | tf_op jit(solution)/shard_map/while/body/eval_jaxpr/ppermute | solution.py:30
  118.3 3.6 multiply_add_fusion.6
  123.0 4.8 %collective-permute-start.8 = (f32[1,1,16,256]{3,2,1,0:T(8,128)S(1)}, f32[1,1,16,256]{3,2,1,0:T(8,128)S(1)}, u32[]{:S(2)}, u32[]{:S(2)}) collective-permute-start(f32[1,1,16,256]{3,2,1,0:T(8,128)S(1)} %get-tuple-element.831), channel_id=1, source_target_pairs={{0,1},{1,2},{2,3},{3,4},{4,5},{5,6},{6,7},{8,9},{9,10},{10,11},{11... | collective-permute-start | bytes 49160 | tf_op jit(solution)/shard_map/ppermute | solution.py:30
  130.2 1.7 add.635
  133.3 3.9 broadcast_multiply_fusion.5
  137.3 76.5 %while.64 = (s32[]{:T(128)}, f32[8,16,16,256]{3,2,1,0:T(8,128)}, f32[8,16,16,256]{3,2,1,0:T(8,128)}, f32[8,16,16,256]{3,2,1,0:T(8,128)}, f32[16,16,256]{2,1,0:T(...) while((s32[]{:T(128)}, f32[8,16,16,256]{3,2,1,0:T(8,128)}, ...), condition=%wide.region_4.5_spmd.clone.clone, body=%wide.region_3.4_spmd.sunk.clone.clone.sunk | while | flops 14811139 | bytes 23068904 | solution.py:143
  139.6 4.5 collective-permute-start.2
  147.9 7.1 %multiply_add_fusion.7 = (f32[8,16,16,256]{3,2,1,0:T(8,128)}, f32[8,16,16,256]{3,2,1,0:T(8,128)}, f32[8,16,16,256]{3,2,1,0:T(8,128)}) fusion(f32[8,16,16,256]{3,2,1,0:T(8,128)S(1)} %copy.49, f32[]{:T(128)} %bitcast.98, f32[]{:T(128)} %bitcast.99, f32[8,16,16,256]{3,2,1,0:T(8,128)} %get-tuple-element.1066, f32[16,16,256]{2,1,0:T(8,128)S(1)} %get-tuple-element.991, ...), kind=kLoop, calls=%fused_computation.69.clone.1 | loop fusion | flops 14155776 | bytes 14417929 | tf_op jit(solution)/shard_map/while/body/eval_jaxpr/add | solution.py:140
  155.0 1.6 copy.49
  157.3 6.1 %collective-permute-start.2 = (f32[8,1,16,256]{3,2,1,0:T(8,128)}, f32[8,1,16,256]{3,2,1,0:T(8,128)}, u32[]{:S(2)}, u32[]{:S(2)}) collective-permute-start(f32[8,1,16,256]{3,2,1,0:T(8,128)} %get-tuple-element.995), channel_id=1, source_target_pairs={{0,1},{1,2},{2,3},{3,4},{4,5},{5,6},{6,7},{8,9},{9,10},{10,11},{11... | collective-permute-start | bytes 393224 | tf_op jit(solution)/shard_map/while/body/eval_jaxpr/ppermute | solution.py:30
  167.0 7.5 %multiply_add_fusion.7 = (f32[8,16,16,256]{3,2,1,0:T(8,128)}, f32[8,16,16,256]{3,2,1,0:T(8,128)}, f32[8,16,16,256]{3,2,1,0:T(8,128)}) fusion(f32[8,16,16,256]{3,2,1,0:T(8,128)S(1)} %copy.49, f32[]{:T(128)} %bitcast.98, f32[]{:T(128)} %bitcast.99, f32[8,16,16,256]{3,2,1,0:T(8,128)} %get-tuple-element.1066, f32[16,16,256]{2,1,0:T(8,128)S(1)} %get-tuple-element.991, ...), kind=kLoop, calls=%fused_computation.69.clone.1 | loop fusion | flops 14155776 | bytes 14417929 | tf_op jit(solution)/shard_map/while/body/eval_jaxpr/add | solution.py:140
  174.5 1.6 copy.49
  176.8 6.7 %collective-permute-start.2 = (f32[8,1,16,256]{3,2,1,0:T(8,128)}, f32[8,1,16,256]{3,2,1,0:T(8,128)}, u32[]{:S(2)}, u32[]{:S(2)}) collective-permute-start(f32[8,1,16,256]{3,2,1,0:T(8,128)} %get-tuple-element.995), channel_id=1, source_target_pairs={{0,1},{1,2},{2,3},{3,4},{4,5},{5,6},{6,7},{8,9},{9,10},{10,11},{11... | collective-permute-start | bytes 393224 | tf_op jit(solution)/shard_map/while/body/eval_jaxpr/ppermute | solution.py:30
  187.1 7.5 %multiply_add_fusion.7 = (f32[8,16,16,256]{3,2,1,0:T(8,128)}, f32[8,16,16,256]{3,2,1,0:T(8,128)}, f32[8,16,16,256]{3,2,1,0:T(8,128)}) fusion(f32[8,16,16,256]{3,2,1,0:T(8,128)S(1)} %copy.49, f32[]{:T(128)} %bitcast.98, f32[]{:T(128)} %bitcast.99, f32[8,16,16,256]{3,2,1,0:T(8,128)} %get-tuple-element.1066, f32[16,16,256]{2,1,0:T(8,128)S(1)} %get-tuple-element.991, ...), kind=kLoop, calls=%fused_computation.69.clone.1 | loop fusion | flops 14155776 | bytes 14417929 | tf_op jit(solution)/shard_map/while/body/eval_jaxpr/add | solution.py:140
  194.6 1.6 copy.49
  196.9 5.8 %collective-permute-start.2 = (f32[8,1,16,256]{3,2,1,0:T(8,128)}, f32[8,1,16,256]{3,2,1,0:T(8,128)}, u32[]{:S(2)}, u32[]{:S(2)}) collective-permute-start(f32[8,1,16,256]{3,2,1,0:T(8,128)} %get-tuple-element.995), channel_id=1, source_target_pairs={{0,1},{1,2},{2,3},{3,4},{4,5},{5,6},{6,7},{8,9},{9,10},{10,11},{11... | collective-permute-start | bytes 393224 | tf_op jit(solution)/shard_map/while/body/eval_jaxpr/ppermute | solution.py:30
  206.3 7.5 %multiply_add_fusion.7 = (f32[8,16,16,256]{3,2,1,0:T(8,128)}, f32[8,16,16,256]{3,2,1,0:T(8,128)}, f32[8,16,16,256]{3,2,1,0:T(8,128)}) fusion(f32[8,16,16,256]{3,2,1,0:T(8,128)S(1)} %copy.49, f32[]{:T(128)} %bitcast.98, f32[]{:T(128)} %bitcast.99, f32[8,16,16,256]{3,2,1,0:T(8,128)} %get-tuple-element.1066, f32[16,16,256]{2,1,0:T(8,128)S(1)} %get-tuple-element.991, ...), kind=kLoop, calls=%fused_computation.69.clone.1 | loop fusion | flops 14155776 | bytes 14417929 | tf_op jit(solution)/shard_map/while/body/eval_jaxpr/add | solution.py:140
  213.8 4.9 %broadcast_multiply_fusion.4 = (f32[8,16,16,256]{3,2,1,0:T(8,128)}, f32[8,16,16,256]{3,2,1,0:T(8,128)}) fusion(f32[16,16,256]{2,1,0:T(8,128)} %add.635, f32[8,16,16,256]{3,2,1,0:T(8,128)} %get-tuple-element.571, f32[8,16,16,256]{3,2,1,0:T(8,128)} %get-tuple-element.572), kind=kLoop, calls=%fused_computation.180 | loop fusion | flops 1572864 | bytes 8650752 | tf_op jit(solution)/shard_map/mul | solution.py:132
  218.7 76.2 %while.65 = (s32[]{:T(128)}, f32[8,16,16,256]{3,2,1,0:T(8,128)}, f32[8,16,16,256]{3,2,1,0:T(8,128)}, f32[8,16,16,256]{3,2,1,0:T(8,128)}, f32[16,16,256]{2,1,0:T(...) while((s32[]{:T(128)}, f32[8,16,16,256]{3,2,1,0:T(8,128)}, ...), condition=%wide.region_7.8_spmd.clone.clone, body=%wide.region_6.7_spmd.sunk.clone.clone.sunk | while | flops 14811139 | bytes 23068904 | solution.py:143
  221.1 5.8 %collective-permute-start.4 = (f32[8,1,16,256]{3,2,1,0:T(8,128)}, f32[8,1,16,256]{3,2,1,0:T(8,128)}, u32[]{:S(2)}, u32[]{:S(2)}) collective-permute-start(f32[8,1,16,256]{3,2,1,0:T(8,128)} %get-tuple-element.1013), channel_id=1, source_target_pairs={{0,1},{1,2},{2,3},{3,4},{4,5},{5,6},{6,7},{8,9},{9,10},{10,11},{11... | collective-permute-start | bytes 393224 | tf_op jit(solution)/shard_map/while/body/eval_jaxpr/ppermute | solution.py:30
  230.5 7.0 %multiply_add_fusion.8 = (f32[8,16,16,256]{3,2,1,0:T(8,128)}, f32[8,16,16,256]{3,2,1,0:T(8,128)}, f32[8,16,16,256]{3,2,1,0:T(8,128)}) fusion(f32[8,16,16,256]{3,2,1,0:T(8,128)S(1)} %copy.50, f32[]{:T(128)} %bitcast.100, f32[]{:T(128)} %bitcast.101, f32[8,16,16,256]{3,2,1,0:T(8,128)} %get-tuple-element.1099, ...), kind=kLoop, calls=%fused_computation.110.clone.1 | loop fusion | flops 14155776 | bytes 14417929 | tf_op jit(solution)/shard_map/while/body/eval_jaxpr/add | solution.py:140
  239.9 5.8 %collective-permute-start.4 = (f32[8,1,16,256]{3,2,1,0:T(8,128)}, f32[8,1,16,256]{3,2,1,0:T(8,128)}, u32[]{:S(2)}, u32[]{:S(2)}) collective-permute-start(f32[8,1,16,256]{3,2,1,0:T(8,128)} %get-tuple-element.1013), channel_id=1, source_target_pairs={{0,1},{1,2},{2,3},{3,4},{4,5},{5,6},{6,7},{8,9},{9,10},{10,11},{11... | collective-permute-start | bytes 393224 | tf_op jit(solution)/shard_map/while/body/eval_jaxpr/ppermute | solution.py:30
  249.3 7.4 %multiply_add_fusion.8 = (f32[8,16,16,256]{3,2,1,0:T(8,128)}, f32[8,16,16,256]{3,2,1,0:T(8,128)}, f32[8,16,16,256]{3,2,1,0:T(8,128)}) fusion(f32[8,16,16,256]{3,2,1,0:T(8,128)S(1)} %copy.50, f32[]{:T(128)} %bitcast.100, f32[]{:T(128)} %bitcast.101, f32[8,16,16,256]{3,2,1,0:T(8,128)} %get-tuple-element.1099, ...), kind=kLoop, calls=%fused_computation.110.clone.1 | loop fusion | flops 14155776 | bytes 14417929 | tf_op jit(solution)/shard_map/while/body/eval_jaxpr/add | solution.py:140
  259.0 5.8 %collective-permute-start.4 = (f32[8,1,16,256]{3,2,1,0:T(8,128)}, f32[8,1,16,256]{3,2,1,0:T(8,128)}, u32[]{:S(2)}, u32[]{:S(2)}) collective-permute-start(f32[8,1,16,256]{3,2,1,0:T(8,128)} %get-tuple-element.1013), channel_id=1, source_target_pairs={{0,1},{1,2},{2,3},{3,4},{4,5},{5,6},{6,7},{8,9},{9,10},{10,11},{11... | collective-permute-start | bytes 393224 | tf_op jit(solution)/shard_map/while/body/eval_jaxpr/ppermute | solution.py:30
  268.4 7.4 %multiply_add_fusion.8 = (f32[8,16,16,256]{3,2,1,0:T(8,128)}, f32[8,16,16,256]{3,2,1,0:T(8,128)}, f32[8,16,16,256]{3,2,1,0:T(8,128)}) fusion(f32[8,16,16,256]{3,2,1,0:T(8,128)S(1)} %copy.50, f32[]{:T(128)} %bitcast.100, f32[]{:T(128)} %bitcast.101, f32[8,16,16,256]{3,2,1,0:T(8,128)} %get-tuple-element.1099, ...), kind=kLoop, calls=%fused_computation.110.clone.1 | loop fusion | flops 14155776 | bytes 14417929 | tf_op jit(solution)/shard_map/while/body/eval_jaxpr/add | solution.py:140
  278.1 5.8 %collective-permute-start.4 = (f32[8,1,16,256]{3,2,1,0:T(8,128)}, f32[8,1,16,256]{3,2,1,0:T(8,128)}, u32[]{:S(2)}, u32[]{:S(2)}) collective-permute-start(f32[8,1,16,256]{3,2,1,0:T(8,128)} %get-tuple-element.1013), channel_id=1, source_target_pairs={{0,1},{1,2},{2,3},{3,4},{4,5},{5,6},{6,7},{8,9},{9,10},{10,11},{11... | collective-permute-start | bytes 393224 | tf_op jit(solution)/shard_map/while/body/eval_jaxpr/ppermute | solution.py:30
  287.6 7.4 %multiply_add_fusion.8 = (f32[8,16,16,256]{3,2,1,0:T(8,128)}, f32[8,16,16,256]{3,2,1,0:T(8,128)}, f32[8,16,16,256]{3,2,1,0:T(8,128)}) fusion(f32[8,16,16,256]{3,2,1,0:T(8,128)S(1)} %copy.50, f32[]{:T(128)} %bitcast.100, f32[]{:T(128)} %bitcast.101, f32[8,16,16,256]{3,2,1,0:T(8,128)} %get-tuple-element.1099, ...), kind=kLoop, calls=%fused_computation.110.clone.1 | loop fusion | flops 14155776 | bytes 14417929 | tf_op jit(solution)/shard_map/while/body/eval_jaxpr/add | solution.py:140
  294.9 2.7 add.636
  297.7 5.2 %collective-permute-start.10 = (f32[8,1,16,256]{3,2,1,0:T(8,128)S(1)}, f32[8,1,16,256]{3,2,1,0:T(8,128)S(1)}, u32[]{:S(2)}, u32[]{:S(2)}) collective-permute-start(f32[8,1,16,256]{3,2,1,0:T(8,128)S(1)} %get-tuple-element.818), channel_id=1, source_target_pairs={{0,1},{1,2},{2,3},{3,4},{4,5},{5,6},{6,7},{8,9},{9,10},{10,11},{11... | collective-permute-start | bytes 393224 | tf_op jit(solution)/shard_map/ppermute | solution.py:30
  304.2 1.9 collective-permute-done.11
  307.9 2.3 fusion.107
  310.2 45.5 %collective-permute-done.12 = f32[8,16,16,256]{3,2,1,0:T(8,128)S(1)} collective-permute-done((f32[8,16,16,256]{3,2,1,0:T(8,128)S(1)}, f32[8,16,16,256]{3,2,1,0:T(8,128)S(1)}, u32[]{:S(2)}, u32[]{:S(2)}) %collective-permute-start.12) | collective-permute-done | bytes 2097184 | tf_op jit(solution)/shard_map/ppermute | solution.py:18
  357.5 92.3 %collective-permute-done.13 = f32[8,16,16,256]{3,2,1,0:T(8,128)} collective-permute-done((f32[8,16,16,256]{3,2,1,0:T(8,128)S(1)}, f32[8,16,16,256]{3,2,1,0:T(8,128)}, u32[]{:S(2)}, u32[]{:S(2)}) %collective-permute-start.13) | collective-permute-done | bytes 2097184 | tf_op jit(solution)/shard_map/ppermute | solution.py:18
  449.8 1.9 dynamic-slice_add_fusion
  (172 shorter events, 73.6 us)
Async XLA Ops:
  6.5 50.8 %all-gather.2.cloned.1.call-start = ((), (), s32[]{:S(2)}) async-start(), calls=%async_computation | async-start | bytes 2621440 | tf_op jit(solution)/shard_map/all_gather | solution.py:112
  9.0 60.8 %copy-start = (f32[1,16,16,256]{3,2,1,0:T(8,128)}, f32[1,16,16,256]{3,2,1,0:T(8,128)S(1)}, u32[]{:S(2)}) copy-start(f32[1,16,16,256]{3,2,1,0:T(8,128)S(1)} %get-tuple-element.823) | copy-start | bytes 786436
  59.3 5.2 %copy-start.13 = (s32[1,8]{1,0:T(1,128)S(1)}, s32[1,8]{1,0:T(1,128)}, u32[]{:S(2)}) copy-start(s32[1,8]{1,0:T(1,128)} %param.16) | copy-start | bytes 100
  59.3 5.2 %copy-start.14 = (f32[1,8]{1,0:T(1,128)S(1)}, f32[1,8]{1,0:T(1,128)}, u32[]{:S(2)}) copy-start(f32[1,8]{1,0:T(1,128)} %param.17) | copy-start | bytes 100
  60.2 7.9 %collective-permute-start.6 = (f32[9,2,16,256]{3,2,1,0:T(8,128)}, f32[9,2,16,256]{3,2,1,0:T(8,128)S(1)}, u32[]{:S(2)}, u32[]{:S(2)}) collective-permute-start(f32[9,2,16,256]{3,2,1,0:T(8,128)} %get-tuple-element.817), channel_id=1, source_target_pairs={{1,0},{2,1},{3,2},{4,3},{5,4},{6,5},{7,6},{9,8},{10,9},{11,10},{12... | collective-permute-start | bytes 884744 | tf_op jit(solution)/shard_map/ppermute | solution.py:32
  61.5 6.6 %collective-permute-start.7 = (f32[9,2,16,256]{3,2,1,0:T(8,128)}, f32[9,2,16,256]{3,2,1,0:T(8,128)S(1)}, u32[]{:S(2)}, u32[]{:S(2)}) collective-permute-start(f32[9,2,16,256]{3,2,1,0:T(8,128)} %get-tuple-element.816), channel_id=1, source_target_pairs={{0,1},{1,2},{2,3},{3,4},{4,5},{5,6},{6,7},{8,9},{9,10},{10,11},{11... | collective-permute-start | bytes 884744 | tf_op jit(solution)/shard_map/ppermute | solution.py:30
  68.1 2.6 copy-start.2
  69.9 0.8 copy-start.15
  71.7 5.9 %collective-permute-start = (f32[1,1,16,256]{3,2,1,0:T(8,128)S(1)}, f32[1,1,16,256]{3,2,1,0:T(8,128)S(1)}, u32[]{:S(2)}, u32[]{:S(2)}) collective-permute-start(f32[1,1,16,256]{3,2,1,0:T(8,128)S(1)} %get-tuple-element.979), channel_id=1, source_target_pairs={{0,1},{1,2},{2,3},{3,4},{4,5},{5,6},{6,7},{8,9},{9,10},{10,11},{11... | collective-permute-start | bytes 49160 | tf_op jit(solution)/shard_map/while/body/eval_jaxpr/ppermute | solution.py:30
  75.0 5.0 %collective-permute-start.1 = (f32[1,1,16,256]{3,2,1,0:T(8,128)S(1)}, f32[1,1,16,256]{3,2,1,0:T(8,128)S(1)}, u32[]{:S(2)}, u32[]{:S(2)}) collective-permute-start(f32[1,1,16,256]{3,2,1,0:T(8,128)S(1)} %get-tuple-element.980), channel_id=1, source_target_pairs={{1,0},{2,1},{3,2},{4,3},{5,4},{6,5},{7,6},{9,8},{10,9},{11,10},{12... | collective-permute-start | bytes 49160 | tf_op jit(solution)/shard_map/while/body/eval_jaxpr/ppermute | solution.py:32
  84.5 7.0 %collective-permute-start = (f32[1,1,16,256]{3,2,1,0:T(8,128)S(1)}, f32[1,1,16,256]{3,2,1,0:T(8,128)S(1)}, u32[]{:S(2)}, u32[]{:S(2)}) collective-permute-start(f32[1,1,16,256]{3,2,1,0:T(8,128)S(1)} %get-tuple-element.979), channel_id=1, source_target_pairs={{0,1},{1,2},{2,3},{3,4},{4,5},{5,6},{6,7},{8,9},{9,10},{10,11},{11... | collective-permute-start | bytes 49160 | tf_op jit(solution)/shard_map/while/body/eval_jaxpr/ppermute | solution.py:30
  88.8 3.3 collective-permute-start.1
  96.7 8.6 %collective-permute-start = (f32[1,1,16,256]{3,2,1,0:T(8,128)S(1)}, f32[1,1,16,256]{3,2,1,0:T(8,128)S(1)}, u32[]{:S(2)}, u32[]{:S(2)}) collective-permute-start(f32[1,1,16,256]{3,2,1,0:T(8,128)S(1)} %get-tuple-element.979), channel_id=1, source_target_pairs={{0,1},{1,2},{2,3},{3,4},{4,5},{5,6},{6,7},{8,9},{9,10},{10,11},{11... | collective-permute-start | bytes 49160 | tf_op jit(solution)/shard_map/while/body/eval_jaxpr/ppermute | solution.py:30
  102.7 3.1 collective-permute-start.1
  110.4 7.4 %collective-permute-start = (f32[1,1,16,256]{3,2,1,0:T(8,128)S(1)}, f32[1,1,16,256]{3,2,1,0:T(8,128)S(1)}, u32[]{:S(2)}, u32[]{:S(2)}) collective-permute-start(f32[1,1,16,256]{3,2,1,0:T(8,128)S(1)} %get-tuple-element.979), channel_id=1, source_target_pairs={{0,1},{1,2},{2,3},{3,4},{4,5},{5,6},{6,7},{8,9},{9,10},{10,11},{11... | collective-permute-start | bytes 49160 | tf_op jit(solution)/shard_map/while/body/eval_jaxpr/ppermute | solution.py:30
  115.2 3.1 collective-permute-start.1
  123.0 8.9 %collective-permute-start.8 = (f32[1,1,16,256]{3,2,1,0:T(8,128)S(1)}, f32[1,1,16,256]{3,2,1,0:T(8,128)S(1)}, u32[]{:S(2)}, u32[]{:S(2)}) collective-permute-start(f32[1,1,16,256]{3,2,1,0:T(8,128)S(1)} %get-tuple-element.831), channel_id=1, source_target_pairs={{0,1},{1,2},{2,3},{3,4},{4,5},{5,6},{6,7},{8,9},{9,10},{10,11},{11... | collective-permute-start | bytes 49160 | tf_op jit(solution)/shard_map/ppermute | solution.py:30
  127.8 4.1 collective-permute-start.9
  131.9 1.4 copy-start.1
  131.9 1.4 copy-start.3
  131.9 1.4 copy-start.5
  139.6 8.0 %collective-permute-start.2 = (f32[8,1,16,256]{3,2,1,0:T(8,128)}, f32[8,1,16,256]{3,2,1,0:T(8,128)}, u32[]{:S(2)}, u32[]{:S(2)}) collective-permute-start(f32[8,1,16,256]{3,2,1,0:T(8,128)} %get-tuple-element.995), channel_id=1, source_target_pairs={{0,1},{1,2},{2,3},{3,4},{4,5},{5,6},{6,7},{8,9},{9,10},{10,11},{11... | collective-permute-start | bytes 393224 | tf_op jit(solution)/shard_map/while/body/eval_jaxpr/ppermute | solution.py:30
  144.1 3.8 collective-permute-start.3
  157.3 9.6 %collective-permute-start.2 = (f32[8,1,16,256]{3,2,1,0:T(8,128)}, f32[8,1,16,256]{3,2,1,0:T(8,128)}, u32[]{:S(2)}, u32[]{:S(2)}) collective-permute-start(f32[8,1,16,256]{3,2,1,0:T(8,128)} %get-tuple-element.995), channel_id=1, source_target_pairs={{0,1},{1,2},{2,3},{3,4},{4,5},{5,6},{6,7},{8,9},{9,10},{10,11},{11... | collective-permute-start | bytes 393224 | tf_op jit(solution)/shard_map/while/body/eval_jaxpr/ppermute | solution.py:30
  163.4 3.6 collective-permute-start.3
  176.8 10.3 %collective-permute-start.2 = (f32[8,1,16,256]{3,2,1,0:T(8,128)}, f32[8,1,16,256]{3,2,1,0:T(8,128)}, u32[]{:S(2)}, u32[]{:S(2)}) collective-permute-start(f32[8,1,16,256]{3,2,1,0:T(8,128)} %get-tuple-element.995), channel_id=1, source_target_pairs={{0,1},{1,2},{2,3},{3,4},{4,5},{5,6},{6,7},{8,9},{9,10},{10,11},{11... | collective-permute-start | bytes 393224 | tf_op jit(solution)/shard_map/while/body/eval_jaxpr/ppermute | solution.py:30
  183.5 3.6 collective-permute-start.3
  196.9 9.4 %collective-permute-start.2 = (f32[8,1,16,256]{3,2,1,0:T(8,128)}, f32[8,1,16,256]{3,2,1,0:T(8,128)}, u32[]{:S(2)}, u32[]{:S(2)}) collective-permute-start(f32[8,1,16,256]{3,2,1,0:T(8,128)} %get-tuple-element.995), channel_id=1, source_target_pairs={{0,1},{1,2},{2,3},{3,4},{4,5},{5,6},{6,7},{8,9},{9,10},{10,11},{11... | collective-permute-start | bytes 393224 | tf_op jit(solution)/shard_map/while/body/eval_jaxpr/ppermute | solution.py:30
  202.7 3.6 collective-permute-start.3
  221.1 9.4 %collective-permute-start.4 = (f32[8,1,16,256]{3,2,1,0:T(8,128)}, f32[8,1,16,256]{3,2,1,0:T(8,128)}, u32[]{:S(2)}, u32[]{:S(2)}) collective-permute-start(f32[8,1,16,256]{3,2,1,0:T(8,128)} %get-tuple-element.1013), channel_id=1, source_target_pairs={{0,1},{1,2},{2,3},{3,4},{4,5},{5,6},{6,7},{8,9},{9,10},{10,11},{11... | collective-permute-start | bytes 393224 | tf_op jit(solution)/shard_map/while/body/eval_jaxpr/ppermute | solution.py:30
  226.9 3.6 collective-permute-start.5
  239.9 9.4 %collective-permute-start.4 = (f32[8,1,16,256]{3,2,1,0:T(8,128)}, f32[8,1,16,256]{3,2,1,0:T(8,128)}, u32[]{:S(2)}, u32[]{:S(2)}) collective-permute-start(f32[8,1,16,256]{3,2,1,0:T(8,128)} %get-tuple-element.1013), channel_id=1, source_target_pairs={{0,1},{1,2},{2,3},{3,4},{4,5},{5,6},{6,7},{8,9},{9,10},{10,11},{11... | collective-permute-start | bytes 393224 | tf_op jit(solution)/shard_map/while/body/eval_jaxpr/ppermute | solution.py:30
  245.7 3.6 collective-permute-start.5
  259.0 9.4 %collective-permute-start.4 = (f32[8,1,16,256]{3,2,1,0:T(8,128)}, f32[8,1,16,256]{3,2,1,0:T(8,128)}, u32[]{:S(2)}, u32[]{:S(2)}) collective-permute-start(f32[8,1,16,256]{3,2,1,0:T(8,128)} %get-tuple-element.1013), channel_id=1, source_target_pairs={{0,1},{1,2},{2,3},{3,4},{4,5},{5,6},{6,7},{8,9},{9,10},{10,11},{11... | collective-permute-start | bytes 393224 | tf_op jit(solution)/shard_map/while/body/eval_jaxpr/ppermute | solution.py:30
  264.8 3.6 collective-permute-start.5
  278.1 9.4 %collective-permute-start.4 = (f32[8,1,16,256]{3,2,1,0:T(8,128)}, f32[8,1,16,256]{3,2,1,0:T(8,128)}, u32[]{:S(2)}, u32[]{:S(2)}) collective-permute-start(f32[8,1,16,256]{3,2,1,0:T(8,128)} %get-tuple-element.1013), channel_id=1, source_target_pairs={{0,1},{1,2},{2,3},{3,4},{4,5},{5,6},{6,7},{8,9},{9,10},{10,11},{11... | collective-permute-start | bytes 393224 | tf_op jit(solution)/shard_map/while/body/eval_jaxpr/ppermute | solution.py:30
  283.9 3.6 collective-permute-start.5
  297.7 6.5 %collective-permute-start.10 = (f32[8,1,16,256]{3,2,1,0:T(8,128)S(1)}, f32[8,1,16,256]{3,2,1,0:T(8,128)S(1)}, u32[]{:S(2)}, u32[]{:S(2)}) collective-permute-start(f32[8,1,16,256]{3,2,1,0:T(8,128)S(1)} %get-tuple-element.818), channel_id=1, source_target_pairs={{0,1},{1,2},{2,3},{3,4},{4,5},{5,6},{6,7},{8,9},{9,10},{10,11},{11... | collective-permute-start | bytes 393224 | tf_op jit(solution)/shard_map/ppermute | solution.py:30
  302.8 3.2 collective-permute-start.11
  306.4 1.0 copy-start.6
  306.4 1.0 copy-start.7
  306.4 1.1 copy-start.8
  306.5 1.2 copy-start.9
  306.5 1.2 copy-start.10
  306.5 1.3 copy-start.11
  306.5 1.4 copy-start.12
  310.1 45.6 %collective-permute-start.12 = (f32[8,16,16,256]{3,2,1,0:T(8,128)S(1)}, f32[8,16,16,256]{3,2,1,0:T(8,128)S(1)}, u32[]{:S(2)}, u32[]{:S(2)}) collective-permute-start(f32[8,16,16,256]{3,2,1,0:T(8,128)S(1)} %fusion.107), channel_id=1, source_target_pairs={{0,8},{8,0},{16,24},{24,16},{1,9},{9,1},{17,25},{25,17},{2,10},{10... | collective-permute-start | bytes 6291464 | tf_op jit(solution)/shard_map/ppermute | solution.py:18
  356.2 93.6 %collective-permute-start.13 = (f32[8,16,16,256]{3,2,1,0:T(8,128)S(1)}, f32[8,16,16,256]{3,2,1,0:T(8,128)}, u32[]{:S(2)}, u32[]{:S(2)}) collective-permute-start(f32[8,16,16,256]{3,2,1,0:T(8,128)S(1)} %add.642), channel_id=1, source_target_pairs={{0,16},{8,24},{16,0},{24,8},{1,17},{9,25},{17,1},{25,9},{2,18},{10... | collective-permute-start | bytes 6291464 | tf_op jit(solution)/shard_map/ppermute | solution.py:18
  (2 other events, 1.6 us)
Sparse Core Ops, SparseCore 0:
  8.9 48.3 all-gather.1
